TPU v7x, 512 devices: a whole 4x8x8 slice. The times are simulated.
512 devices in a mesh: seq: 16 (over z, core), expert: 32 (over x, y).
Axes of the slice: x: 4, y: 8, z: 8, core: 2. Of those that a mesh axis runs over, the one named last changes fastest.
Arguments:
- hidden: bfloat16 [32, 1024, 2048], P('expert', 'seq'), may hold values from -6 to 6
- queries: bfloat16 [32, 1024, 4608], P('expert', 'seq'), may hold values from -5 to 5
- suffix_latent: bfloat16 [32, 1024, 576], P('expert', 'seq'), may hold values from -6 to 6
- prefix_latent: bfloat16 [2, 1024, 576], P(None, 'seq'), may hold values from -6 to 6
- lengths: int32 [32, 4], P('expert'), may hold values from 1 to 512, 1024 in all within a row
- prefix_of: int32 [32, 4], P('expert'), may hold values from 0 to 1
- value_up: bfloat16 [8, 512, 128], replicated, may hold values from -1 to 1
- out_proj: bfloat16 [1024, 2048], P(None, 'expert'), may hold values from -0.1875 to 0.1875
- norm_gain: float32 [2048], replicated, may hold values from 0.5 to 1.5
- router: bfloat16 [2048, 32], replicated, may hold values from -0.0625 to 0.0625
- routes: int32 [32, 1024, 6], P('expert', 'seq'), may hold values from 0 to 31, all different within a row; in each aligned block of 64 rows (0 to 63, 64 to 127, ..., all dimensions but the last counted through in order) at most 16 rows name the same one
- expert_in: bfloat16 [32, 2048, 1408], P('expert', 'seq'), may hold values from -0.125 to 0.125
- expert_out: bfloat16 [32, 2048, 704], P('expert', 'seq'), may hold values from -1.25 to 1.25
Outputs:
- layer_out: bfloat16 [32, 1024, 2048], P('expert', 'seq')
Inputs may be any that keep to these rules, and one draw needn't show every extreme that they name: `routes`: among the rows of one device (aligned blocks of 64 tokens) no expert is named more than 16 times, a bound that some block reaches; a token's 6 experts differ. `lengths`: each row sums to 1024; its longest request has exactly 512 tokens.
All inputs are finite; a program needn't handle non-finite values.
Results may differ from a plain program's by a relative error of at most 0.013.
Values may be sent and summed in bfloat16 or wider, within the bound.
No kernel may reach another device: no remote copies, remote signals or barrier semaphores. Data moves between devices by JAX's collectives and lax.ppermute only.
A program may use at most 128 MiB of HBM per device.

v0:
```python
import jax
import jax.numpy as jnp
from jax import lax
from jax.sharding import PartitionSpec as P

qk_scale = 192.0 ** (-0.5)
big_negative = -1e30


def request_of(positions, request_ends):
    return jnp.sum((positions[:, None] >= request_ends[None, :]).astype(jnp.int32), axis=1)


def merge_scores(running, scores, allowed, values):
    running_max, running_sum, running_acc = running
    new_max = jnp.maximum(running_max, jnp.max(jnp.where(allowed, scores, big_negative), axis=2))
    weights = jnp.where(allowed, jnp.exp(scores - new_max[:, :, None]), 0.0)
    new_sum = jnp.sum(weights, axis=2)
    new_acc = jnp.einsum(
        "thn,nl->thl", weights.astype(jnp.bfloat16), values, preferred_element_type=jnp.float32
    )
    return (new_max, new_sum, new_acc)


def local(
    hidden,
    queries,
    suffix_latent,
    prefix_latent,
    lengths,
    prefix_of,
    value_up,
    out_proj,
    norm_gain,
    router,
    routes,
    expert_in,
    expert_out,
):
    local_tokens = hidden.shape[1]
    model_width = hidden.shape[2]
    key_width = suffix_latent.shape[2]
    head_count = value_up.shape[0]
    latent_width = value_up.shape[1]
    expert_count = router.shape[1]
    top_count = routes.shape[2]
    capacity = 4 * local_tokens * top_count // (3 * expert_count)
    request_count = lengths.shape[1]
    request_ends = jnp.cumsum(lengths[0])
    my_positions = lax.axis_index("seq") * local_tokens + jnp.arange(local_tokens, dtype=jnp.int32)
    my_requests = request_of(my_positions, request_ends)
    request_ids = jnp.arange(request_count, dtype=jnp.int32)
    chosen = jnp.sum(
        jnp.where(my_requests[:, None] == request_ids[None, :], prefix_of[0][None, :], 0), axis=1
    )
    prefix_pick = chosen[:, None] == jnp.arange(2, dtype=jnp.int32)[None, :]
    single_prefix = jnp.all(chosen == chosen[0])
    my_prefix = chosen[0]
    query_rows = queries[0].reshape(local_tokens, head_count, key_width)
    start_state = (
        jnp.full((local_tokens, head_count), big_negative, jnp.float32),
        jnp.zeros((local_tokens, head_count), jnp.float32),
        jnp.zeros((local_tokens, head_count, latent_width), jnp.float32),
    )
    suffix_piece = lax.all_gather(suffix_latent, "seq", axis=1, tiled=True)
    prefix_piece = lax.all_gather(prefix_latent, "seq", axis=1, tiled=True)
    piece_rows = suffix_piece.shape[1]
    suffix_keys = suffix_piece[0]
    key_positions = jnp.arange(piece_rows, dtype=jnp.int32)
    key_requests = request_of(key_positions, request_ends)
    suffix_allowed = (key_requests[None, :] == my_requests[:, None]) & (
        key_positions[None, :] <= my_positions[:, None]
    )
    suffix_scores = (
        jnp.einsum("thk,nk->thn", query_rows, suffix_keys, preferred_element_type=jnp.float32)
        * qk_scale
    )

    def one_prefix(running_state):
        chosen_keys = lax.dynamic_index_in_dim(prefix_piece, my_prefix, 0, keepdims=False)
        prefix_scores = (
            jnp.einsum("thk,nk->thn", query_rows, chosen_keys, preferred_element_type=jnp.float32)
            * qk_scale
        )
        scores = jnp.concatenate([suffix_scores, prefix_scores], axis=2)
        every_key = jnp.ones((local_tokens, piece_rows), dtype=bool)
        allowed = jnp.concatenate([suffix_allowed, every_key], axis=1)[:, None, :]
        values = jnp.concatenate(
            [suffix_keys[:, :latent_width], chosen_keys[:, :latent_width]], axis=0
        )
        return merge_scores(running_state, scores, allowed, values)

    def two_prefixes(running_state):
        prefix_scores = (
            jnp.einsum(
                "thk,pnk->thpn", query_rows, prefix_piece, preferred_element_type=jnp.float32
            )
            * qk_scale
        )
        scores = jnp.concatenate(
            [suffix_scores, prefix_scores.reshape(local_tokens, head_count, 2 * piece_rows)], axis=2
        )
        prefix_allowed = jnp.broadcast_to(
            prefix_pick[:, :, None], (local_tokens, 2, piece_rows)
        ).reshape(local_tokens, 2 * piece_rows)
        allowed = jnp.concatenate([suffix_allowed, prefix_allowed], axis=1)[:, None, :]
        values = jnp.concatenate(
            [
                suffix_keys[:, :latent_width],
                prefix_piece[:, :, :latent_width].reshape(2 * piece_rows, latent_width),
            ],
            axis=0,
        )
        return merge_scores(running_state, scores, allowed, values)

    final_max, final_sum, final_acc = lax.cond(single_prefix, one_prefix, two_prefixes, start_state)
    latent_out = (final_acc / final_sum[:, :, None]).astype(jnp.bfloat16)
    value_out = jnp.einsum(
        "thl,hlv->thv", latent_out, value_up, preferred_element_type=jnp.float32
    ).astype(jnp.bfloat16)
    value_out = value_out.reshape(local_tokens, head_count * value_up.shape[2])
    projected = jnp.dot(
        value_out,
        lax.all_gather(out_proj, "expert", axis=1, tiled=True),
        preferred_element_type=jnp.float32,
    )
    residual = hidden[0].astype(jnp.float32) + projected
    normed = (
        residual
        * lax.rsqrt(jnp.mean(residual * residual, axis=1, keepdims=True) + 1e-06)
        * norm_gain
    ).astype(jnp.bfloat16)
    logits = jnp.dot(normed, router, preferred_element_type=jnp.float32)
    expert_probs = jax.nn.softmax(logits, axis=1)
    expert_ids = jnp.arange(expert_count, dtype=jnp.int32)
    my_routes = routes[0]
    matches = my_routes[:, :, None] == expert_ids[None, None, :]
    gate_values = jnp.sum(jnp.where(matches, expert_probs[:, None, :], 0.0), axis=2)
    flat_hits = matches.reshape(local_tokens * top_count, expert_count).astype(jnp.int32)
    earlier = jnp.cumsum(flat_hits, axis=0) - flat_hits
    slot_index = jnp.sum(earlier * flat_hits, axis=1).reshape(local_tokens, top_count)
    cell_index = my_routes * capacity + slot_index
    cell_ids = jnp.arange(expert_count * capacity, dtype=jnp.int32)
    placing = jnp.sum(
        (cell_ids[:, None, None] == cell_index[None, :, :]).astype(jnp.int32), axis=2
    ).astype(jnp.bfloat16)
    outgoing = jnp.dot(placing, normed, preferred_element_type=jnp.float32).astype(jnp.bfloat16)
    outgoing = outgoing.reshape(expert_count, capacity, model_width)
    incoming = lax.all_to_all(outgoing, "expert", split_axis=0, concat_axis=0, tiled=True)
    full_in, full_out = (
        lax.all_gather(expert_in, "seq", axis=1, tiled=True),
        lax.all_gather(expert_out, "seq", axis=1, tiled=True),
    )
    all_rows = incoming.reshape(-1, model_width)
    gate_up = jnp.dot(all_rows, full_in[0], preferred_element_type=jnp.float32)
    hidden_units = gate_up.shape[1] // 2
    active = (jax.nn.silu(gate_up[:, :hidden_units]) * gate_up[:, hidden_units:]).astype(
        jnp.bfloat16
    )
    produced = lax.dot_general(
        active, full_out[0], (((1,), (1,)), ((), ())), preferred_element_type=jnp.float32
    ).astype(jnp.bfloat16)
    returned = lax.all_to_all(
        produced.reshape(-1, capacity, model_width),
        "expert",
        split_axis=0,
        concat_axis=0,
        tiled=True,
    )
    returned_rows = returned.reshape(-1, model_width)
    picked = returned_rows[cell_index]
    routed_sum = jnp.sum(gate_values[:, :, None] * picked.astype(jnp.float32), axis=1)
    layer_out = (residual + routed_sum).astype(jnp.bfloat16)
    return layer_out[None]


def solution(mesh):
    in_specs = (
        P("expert", "seq", None),
        P("expert", "seq", None),
        P("expert", "seq", None),
        P(None, "seq", None),
        P("expert", None),
        P("expert", None),
        P(),
        P(None, "expert"),
        P(),
        P(),
        P("expert", "seq", None),
        P("expert", "seq", None),
        P("expert", "seq", None),
    )
    out_specs = P("expert", "seq", None)
    return jax.shard_map(local, mesh=mesh, in_specs=in_specs, out_specs=out_specs, check_vma=False)
```

profile of v0, /device:TPU:16, one launch (start us, length us, event | category | flops | bytes accessed | tf_op | source)
XLA Modules:
  0.0 368.0 jit_solution(16596417180253832410)
XLA Ops:
  7.3 1.8 copy.86
  13.9 2.4 reshape_squeeze.3
  20.0 36.3 %all-gather.8.cloned.1.call-done = bf16[1,1024,576]{2,1,0:T(8,128)(2,1)} async-done(((bf16[1,64,576]{2,1,0:T(8,128)(2,1)}), bf16[1,1024,576]{2,1,0:T(8,128)(2,1)}) %all-gather.8.cloned.1.call-update) | async-done | bytes 1179664 | tf_op jit(solution)/shard_map/all_gather | solution.py:65
  56.3 2.4 copy.87
  58.7 2.5 convolution_multiply_fusion
  61.3 39.0 %all-gather.6.cloned.1.call-done = bf16[2,1024,576]{2,0,1:T(2,128)(2,1)} async-done(((bf16[2,64,576]{2,0,1:T(2,128)(2,1)}), bf16[2,1024,576]{2,0,1:T(2,128)(2,1)}) %all-gather.6.cloned.1.call-update) | async-done | bytes 2359312 | tf_op jit(solution)/shard_map/all_gather | solution.py:66
  100.3 31.3 %conditional.1 = (f32[64,8,512]{2,1,0:T(8,128)}, f32[64,8]{1,0:T(8,128)S(1)}) conditional(s32[]{:T(128)} %convert_element_type.64, (s32[64]{0:T(128)S(1)}, s32[64,2]{1,0:T(8,128)S(1)}, pred[64,1024]{1,0:T(8,128)(4,1)S(1)}, bf16[64,8,576]{2,1,0:T(8,128)(2,1)}, bf16[2,1024,576]{2,0,1:T(2,128)(2,1)}, /*index=5*/f32[64,8,1024]{2,1,0:T(8,128)S(1)}, ...), branch_computations={%region_5.8_spmd, %region_8.11_spmd} | conditional | flops 2843409920 | bytes 92157032 | solution.py:116
  100.3 7.4 %copy.88 = bf16[2,1024,576]{1,2,0:T(8,128)(2,1)} copy(bf16[2,1024,576]{2,0,1:T(2,128)(2,1)} %get-tuple-element.110) | data formatting | bytes 4718592 | tf_op jit(solution)/shard_map
  107.6 3.7 fusion.10
  111.7 1.2 select_reduce_fusion
  114.5 1.5 slice.36
  116.0 4.0 %copy.82 = bf16[2,1024,512]{2,1,0:T(8,128)(2,1)} copy(bf16[2,1024,512]{1,2,0:T(8,128)(2,1)} %slice.36) | data formatting | bytes 4194304 | tf_op jit(solution)/shard_map/cond/branch_0_fun/slice | solution.py:110
  120.0 2.4 copy.89
  122.4 1.3 slice.35
  123.7 5.9 %fusion.2 = f32[64,8,512]{2,1,0:T(8,128)} fusion(bf16[2048,512]{1,0:T(8,128)(2,1)} %bitcast.104, bf16[1024,512]{1,0:T(8,128)(2,1)S(1)} %slice.35, f32[64,8,2048]{2,1,0:T(8,128)} %bitcast.98, f32[64,8,1024]{2,1,0:T(8,128)S(1)} %get-tuple-element.36, f32[64,8]{1,0:T(8,128)S(1)} %broadcast_maximum_fusion, pred[64,3072]{1,0:T(8,128)(4,1)S(1)} %pad_add_fusion), kind=kOutput, calls=%fused_computation.7 | convolution fusion | flops 1623195648 | bytes 10684416 | tf_op jit(solution)/shard_map/cond/branch_0_fun/thn,nl->thl/dot_general | solution.py:19
  129.6 1.8 fusion.1
  131.5 1.4 divide_convert_fusion
  133.4 54.2 %all-gather.10.cloned.1.call-done = bf16[1024,2048]{0,1:T(8,128)(2,1)} async-done(((bf16[1024,64]{0,1:T(8,128)(2,1)}), bf16[1024,2048]{0,1:T(8,128)(2,1)}) %all-gather.10.cloned.1.call-update) | async-done | bytes 4194320 | tf_op jit(solution)/shard_map/all_gather | solution.py:124
  187.6 3.7 %multiply_reduce_fusion.1 = (f32[64]{0:T(128)S(1)}, f32[64,2048]{1,0:T(8,128)S(1)}) fusion(bf16[1024,2048]{0,1:T(8,128)(2,1)} %all-gather.10.cloned.1.call-done, bf16[8,8,8,128]{3,2,1,0:T(8,128)(2,1)S(1)} %fusion.33, bf16[1,64,2048]{2,1,0:T(8,128)(2,1)S(1)} %copy-done.9), kind=kOutput, calls=%fused_computation.60 | convolution fusion | flops 268959680 | bytes 5112064 | tf_op jit(solution)/shard_map/dot_general | solution.py:122
  192.1 2.1 convolution_convert_fusion.1
  194.1 7.2 %all-to-all-start = ((bf16[32,16,2048]{2,1,0:T(8,128)(2,1)}), bf16[32,16,2048]{2,1,0:T(8,128)(2,1)S(1)}, u32[]{:S(2)}, u32[]{:S(2)}) async-start(bf16[32,16,2048]{2,1,0:T(8,128)(2,1)} %bitcast.20), calls=%async_computation | async-start | bytes 4194304 | tf_op jit(solution)/shard_map/all_to_all | solution.py:149
  201.3 34.9 %all-gather.12.cloned.1.call-done = bf16[1,2048,1408]{2,1,0:T(8,128)(2,1)} async-done(((bf16[1,128,1408]{2,1,0:T(8,128)(2,1)}), bf16[1,2048,1408]{2,1,0:T(8,128)(2,1)}) %all-gather.12.cloned.1.call-update) | async-done | bytes 5767184 | tf_op jit(solution)/shard_map/all_gather | solution.py:151
  236.2 11.3 %all-to-all-done = bf16[32,16,2048]{2,1,0:T(8,128)(2,1)S(1)} async-done(((bf16[32,16,2048]{2,1,0:T(8,128)(2,1)}), bf16[32,16,2048]{2,1,0:T(8,128)(2,1)S(1)}, u32[]{:S(2)}, u32[]{:S(2)}) %all-to-all-start) | async-done | bytes 2097184 | tf_op jit(solution)/shard_map/all_to_all | solution.py:149
  247.5 7.6 %fusion.28 = f32[512,1408]{1,0:T(8,128)} fusion(bf16[512,2048]{1,0:T(8,128)(2,1)S(1)} %bitcast.103, bf16[1,2048,1408]{2,1,0:T(8,128)(2,1)} %all-gather.12.cloned.1.call-done), kind=kOutput, calls=%fused_computation.40 | convolution fusion | flops 2952790016 | bytes 10747904 | tf_op jit(solution)/shard_map/dot_general | solution.py:155
  255.2 28.3 %all-gather.14.cloned.1.call-done = bf16[1,2048,704]{1,2,0:T(8,128)(2,1)} async-done(((bf16[1,128,704]{1,2,0:T(8,128)(2,1)}), bf16[1,2048,704]{1,2,0:T(8,128)(2,1)}) %all-gather.14.cloned.1.call-update) | async-done | bytes 2883600 | tf_op jit(solution)/shard_map/all_gather | solution.py:152
  283.5 6.0 %convolution_convert_fusion = bf16[512,2048]{1,0:T(8,128)(2,1)} fusion(bf16[1,2048,704]{1,2,0:T(8,128)(2,1)} %all-gather.14.cloned.1.call-done, f32[512,1408]{1,0:T(8,128)} %fusion.28), kind=kOutput, calls=%fused_computation.43 | convolution fusion | flops 1479606272 | bytes 8126464 | tf_op jit(solution)/shard_map/dot_general | solution.py:160
  289.5 10.0 %all-to-all-start.1 = ((bf16[32,16,2048]{2,1,0:T(8,128)(2,1)}), bf16[32,16,2048]{2,1,0:T(8,128)(2,1)S(1)}, u32[]{:S(2)}, u32[]{:S(2)}) async-start(bf16[32,16,2048]{2,1,0:T(8,128)(2,1)} %bitcast.102), calls=%async_computation.1 | async-start | bytes 4194304 | tf_op jit(solution)/shard_map/all_to_all | solution.py:163
  299.8 1.3 fusion.50
  301.3 48.6 %all-to-all-done.1 = bf16[32,16,2048]{2,1,0:T(8,128)(2,1)S(1)} async-done(((bf16[32,16,2048]{2,1,0:T(8,128)(2,1)}), bf16[32,16,2048]{2,1,0:T(8,128)(2,1)S(1)}, u32[]{:S(2)}, u32[]{:S(2)}) %all-to-all-start.1) | async-done | bytes 2097184 | tf_op jit(solution)/shard_map/all_to_all | solution.py:163
  349.9 3.1 gather_fusion
  353.0 3.9 %reshape.155 = f32[64,6,2048]{2,1,0:T(8,128)} reshape(bf16[384,2048]{1,0:T(8,128)(2,1)} %gather_fusion) | data formatting | bytes 4718592 | tf_op jit(solution)/shard_map/convert_element_type | solution.py:172
  356.9 3.8 %multiply_reduce_fusion = f32[64,2048]{1,0:T(8,128)S(1)} fusion(f32[64,6,2048]{2,1,0:T(8,128)} %reshape.155, f32[64,6]{1,0:T(8,128)S(1)} %copy.96), kind=kLoop, calls=%fused_computation.42 | loop fusion | flops 1441792 | bytes 3671552 | tf_op jit(solution)/shard_map/reduce_sum | solution.py:172
  (69 shorter events, 12.9 us)
Async XLA Ops:
  6.5 126.4 %copy-start = (bf16[8,512,128]{2,1,0:T(8,128)(2,1)S(1)}, bf16[8,512,128]{2,1,0:T(8,128)(2,1)}, u32[]{:S(2)}) copy-start(bf16[8,512,128]{2,1,0:T(8,128)(2,1)} %param.21) | copy-start | bytes 3145732
  6.5 49.8 %all-gather.8.cloned.1.call-start = ((), (), s32[]{:S(2)}) async-start(), calls=%async_computation.3 | async-start | bytes 1392640 | tf_op jit(solution)/shard_map/all_gather | solution.py:65
  7.3 93.0 %all-gather.6.cloned.1.call-start = ((), (), s32[]{:S(2)}) async-start(), calls=%async_computation.2 | async-start | bytes 2785280 | tf_op jit(solution)/shard_map/all_gather | solution.py:66
  9.1 178.5 %all-gather.10.cloned.1.call-start = ((), (), s32[]{:S(2)}) async-start(), calls=%async_computation.4 | async-start | bytes 4325376 | tf_op jit(solution)/shard_map/all_gather | solution.py:124
  9.8 226.4 %all-gather.12.cloned.1.call-start = ((), (), s32[]{:S(2)}) async-start(), calls=%async_computation.5 | async-start | bytes 6127616 | tf_op jit(solution)/shard_map/all_gather | solution.py:151
  10.4 273.1 %all-gather.14.cloned.1.call-start = ((), (), s32[]{:S(2)}) async-start(), calls=%async_computation.6 | async-start | bytes 3063808 | tf_op jit(solution)/shard_map/all_gather | solution.py:152
  111.3 2.1 copy-start.1
  111.7 2.7 copy-start.4
  123.7 5.9 %copy-start.2 = (f32[64,8,2,1024]{3,1,2,0:T(8,128)S(1)}, f32[64,8,2,1024]{3,1,2,0:T(8,128)}, u32[]{:S(2)}) copy-start(f32[64,8,2,1024]{3,1,2,0:T(8,128)} %copy-done.1) | copy-start | bytes 12582916 | tf_op jit(solution)/shard_map/cond
  131.5 56.0 %copy-start.9 = (bf16[1,64,2048]{2,1,0:T(8,128)(2,1)S(1)}, bf16[1,64,2048]{2,1,0:T(8,128)(2,1)}, u32[]{:S(2)}) copy-start(bf16[1,64,2048]{2,1,0:T(8,128)(2,1)} %param.15) | copy-start | bytes 786436
  133.3 58.7 %copy-start.8 = (s32[512,64]{0,1:T(8,128)S(1)}, s32[512,64]{0,1:T(8,128)}, u32[]{:S(2)}) copy-start(s32[512,64]{0,1:T(8,128)} %convert_reduce_fusion) | copy-start | bytes 393220
  133.3 58.7 %copy-start.11 = (f32[2048]{0:T(1024)S(1)}, f32[2048]{0:T(1024)}, u32[]{:S(2)}) copy-start(f32[2048]{0:T(1024)} %param.23) | copy-start | bytes 24580
  191.2 0.8 copy-start.5
  194.1 53.4 %all-to-all-start = ((bf16[32,16,2048]{2,1,0:T(8,128)(2,1)}), bf16[32,16,2048]{2,1,0:T(8,128)(2,1)S(1)}, u32[]{:S(2)}, u32[]{:S(2)}) async-start(bf16[32,16,2048]{2,1,0:T(8,128)(2,1)} %bitcast.20), calls=%async_computation | async-start | bytes 4194304 | tf_op jit(solution)/shard_map/all_to_all | solution.py:149
  289.5 10.0 %copy-start.12 = (s32[1,64,6]{1,0,2:T(1,128)S(1)}, s32[1,64,6]{1,0,2:T(1,128)}, u32[]{:S(2)}) copy-start(s32[1,64,6]{1,0,2:T(1,128)} %param.25) | copy-start | bytes 4612
  289.5 10.3 %copy-start.10 = (bf16[2048,32]{0,1:T(8,128)(2,1)S(1)}, bf16[2048,32]{0,1:T(8,128)(2,1)}, u32[]{:S(2)}) copy-start(bf16[2048,32]{0,1:T(8,128)(2,1)} %param.24) | copy-start | bytes 393220
  289.5 60.4 %all-to-all-start.1 = ((bf16[32,16,2048]{2,1,0:T(8,128)(2,1)}), bf16[32,16,2048]{2,1,0:T(8,128)(2,1)S(1)}, u32[]{:S(2)}, u32[]{:S(2)}) async-start(bf16[32,16,2048]{2,1,0:T(8,128)(2,1)} %bitcast.102), calls=%async_computation.1 | async-start | bytes 4194304 | tf_op jit(solution)/shard_map/all_to_all | solution.py:163
  356.9 3.8 %copy-start.6 = (f32[64,2048]{1,0:T(8,128)S(1)}, f32[64,2048]{1,0:T(8,128)}, u32[]{:S(2)}) copy-start(f32[64,2048]{1,0:T(8,128)} %copy-done.5) | copy-start | bytes 1572868
Sparse Core Ops, SparseCore 0:
  9.5 46.7 all-gather.7
  58.4 41.7 all-gather.5
  103.4 84.0 all-gather.9
  189.5 46.6 all-gather.11
  238.1 45.3 all-gather.13
where the time goes:
time: 369 us; the launch traced here: 368 us
  waiting for transfers between devices  255 us (69%)
  local copies, waits for them, and re-layouts  34.7 us (9%)
  matrix products  33.2 us (9%)
  starting transfers between devices  17.3 us (5%)
  between operations  14 us (4%)
  other arithmetic  13.5 us (4%)
    all_gather x1, waiting for transfers between devices, local(): lax.all_gather(out_proj, 'expert', axis=1, tiled=True)  54.2 us
    all_to_all x1, waiting for transfers between devices, local(): lax.all_to_all(produced.reshape(-1, capacity, model_width), 'expert', spl...  48.6 us
    all_gather x1, waiting for transfers between devices, local(): prefix_piece = lax.all_gather(prefix_latent, 'seq', axis=1, tiled=True)  39 us
    all_gather x1, waiting for transfers between devices, local(): suffix_piece = lax.all_gather(suffix_latent, 'seq', axis=1, tiled=True)  36.3 us
    all_gather x1, waiting for transfers between devices, local(): lax.all_gather(expert_in, 'seq', axis=1, tiled=True)  34.9 us
    all_gather x1, waiting for transfers between devices, local(): lax.all_gather(expert_out, 'seq', axis=1, tiled=True)  28.3 us
    all_to_all x1, waiting for transfers between devices, local(): lax.all_to_all(outgoing, 'expert', split_axis=0, concat_axis=0, tiled=True)  11.3 us
    all_to_all x1, starting transfers between devices, local(): lax.all_to_all(produced.reshape(-1, capacity, model_width), 'expert', spl...  9.96 us
  transfers between devices with their start and end apart: 7, of which 7 were waited for; matrix products, arithmetic and copies ran while one was open for 17% of the time, Pallas kernels for 0%

commit v1 on v0

--- a/solution.py
+++ b/solution.py
@@ -148,7 +148,9 @@
     outgoing = outgoing.reshape(expert_count, capacity, model_width)
     incoming = lax.all_to_all(outgoing, "expert", split_axis=0, concat_axis=0, tiled=True)
     full_in, full_out = (
-        lax.all_gather(expert_in, "seq", axis=1, tiled=True),
+        jnp.concatenate(
+            lax.all_to_all(jnp.stack([expert_in] * lax.axis_size("seq")), "seq", 0, 0), axis=1
+        ),
         lax.all_gather(expert_out, "seq", axis=1, tiled=True),
     )
     all_rows = incoming.reshape(-1, model_width)

time: 369 us -> 402 us (1.089)
  the two profiles are of different devices: /device:TPU:16 before, /device:TPU:8 now
where the time goes in v1:
time: 402 us; the launch traced here: 401 us
  waiting for transfers between devices  250 us (62%)
  blocking collectives  53.7 us (13%)
  local copies, waits for them, and re-layouts  28.9 us (7%)
  matrix products  27.3 us (7%)
  starting transfers between devices  16 us (4%)
  between operations  14.1 us (4%)
  other arithmetic  10.8 us (3%)
    all_gather x1, waiting for transfers between devices, local(): prefix_piece = lax.all_gather(prefix_latent, 'seq', axis=1, tiled=True)  86.6 us
    all_gather x1, waiting for transfers between devices, local(): lax.all_gather(out_proj, 'expert', axis=1, tiled=True)  71.1 us
    all_to_all x1, blocking collectives, local(): lax.all_to_all(outgoing, 'expert', split_axis=0, concat_axis=0, tiled=True)  53.7 us
    all_gather x1, waiting for transfers between devices, local(): suffix_piece = lax.all_gather(suffix_latent, 'seq', axis=1, tiled=True)  45.7 us
    all_to_all x1, waiting for transfers between devices, local(): lax.all_to_all(produced.reshape(-1, capacity, model_width), 'expert', spl...  44.7 us
    all_to_all x1, starting transfers between devices, local(): lax.all_to_all(jnp.stack([expert_in] * lax.axis_size('seq')), 'seq', 0, 0)  10.6 us
    another operation x2, local copies, waits for them, and re-layouts  8.61 us
  transfers between devices with their start and end apart: 6, of which 4 were waited for; matrix products, arithmetic and copies ran while one was open for 12% of the time, Pallas kernels for 0%

profile of v1, /device:TPU:8, one launch (start us, length us, event | category | flops | bytes accessed | tf_op | source)
XLA Modules:
  0.0 400.9 jit_solution(3850177149839160743)
XLA Ops:
  7.3 1.8 copy.86
  9.8 4.2 %stack.2 = bf16[16,1,128,1408]{3,2,1,0:T(8,128)(2,1)} broadcast(bf16[128,1408]{1,0:T(8,128)(2,1)} %bitcast.108), dimensions={2,3} | broadcast | bytes 6127616 | tf_op jit(solution)/shard_map/stack | solution.py:152
  14.0 10.6 %all-to-all-start.1 = ((bf16[16,1,128,1408]{3,2,1,0:T(8,128)(2,1)}), bf16[16,1,128,1408]{3,2,1,0:T(8,128)(2,1)}, u32[]{:S(2)}, u32[]{:S(2)}) async-start(bf16[16,1,128,1408]{3,2,1,0:T(8,128)(2,1)} %stack.2), calls=%async_computation.1 | async-start | bytes 11534336 | tf_op jit(solution)/shard_map/all_to_all | solution.py:152
  25.6 1.4 reshape_squeeze.3
  27.3 0.8 compare_reduce_fusion
  28.8 0.9 reduce-window.19
  30.3 0.8 convert_reduce_fusion
  31.2 45.7 %all-gather.7.cloned.1.call-done = bf16[1,1024,576]{2,1,0:T(8,128)(2,1)} async-done(((bf16[1,64,576]{2,1,0:T(8,128)(2,1)}), bf16[1,1024,576]{2,1,0:T(8,128)(2,1)}) %all-gather.7.cloned.1.call-update) | async-done | bytes 1179664 | tf_op jit(solution)/shard_map/all_gather | solution.py:65
  76.9 2.4 copy.87
  79.3 2.5 convolution_multiply_fusion
  81.9 86.6 %all-gather.5.cloned.1.call-done = bf16[2,1024,576]{2,0,1:T(2,128)(2,1)} async-done(((bf16[2,64,576]{2,0,1:T(2,128)(2,1)}), bf16[2,1024,576]{2,0,1:T(2,128)(2,1)}) %all-gather.5.cloned.1.call-update) | async-done | bytes 2359312 | tf_op jit(solution)/shard_map/all_gather | solution.py:66
  168.4 16.9 %conditional.1 = (f32[64,8,512]{2,1,0:T(8,128)}, f32[64,8]{1,0:T(8,128)S(1)}) conditional(s32[]{:T(128)} %convert_element_type.64, (s32[64]{0:T(128)S(1)}, s32[64,2]{1,0:T(8,128)S(1)}, pred[64,1024]{1,0:T(8,128)(4,1)S(1)}, bf16[64,8,576]{2,1,0:T(8,128)(2,1)}, bf16[2,1024,576]{2,0,1:T(2,128)(2,1)}, /*index=5*/f32[64,8,1024]{2,1,0:T(8,128)S(1)}, ...), branch_computations={%region_5.8_spmd, %region_8.11_spmd} | conditional | flops 2843409920 | bytes 92157032 | solution.py:116
  168.6 7.4 %copy.90 = bf16[2,1024,576]{1,2,0:T(8,128)(2,1)} copy(bf16[2,1024,576]{2,0,1:T(2,128)(2,1)} %get-tuple-element.115) | data formatting | bytes 4718592 | tf_op jit(solution)/shard_map
  176.0 2.4 multiply_bitcast_fusion
  178.4 1.2 copy.92
  180.2 1.0 fusion.18
  182.7 2.5 fusion.19
  185.4 1.4 divide_convert_fusion
  187.2 71.1 %all-gather.9.cloned.1.call-done = bf16[1024,2048]{0,1:T(8,128)(2,1)} async-done(((bf16[1024,64]{0,1:T(8,128)(2,1)}), bf16[1024,2048]{0,1:T(8,128)(2,1)}) %all-gather.9.cloned.1.call-update) | async-done | bytes 4194320 | tf_op jit(solution)/shard_map/all_gather | solution.py:124
  258.3 3.7 multiply_reduce_fusion.1
  262.0 0.8 copy-done.5
  262.8 0.8 convolution_convert_fusion.1
  263.6 53.7 %all_to_all.15 = bf16[32,16,2048]{2,1,0:T(8,128)(2,1)S(1)} all-to-all(bf16[32,16,2048]{2,1,0:T(8,128)(2,1)S(1)} %bitcast.102), channel_id=1, replica_groups=mesh['seq'=16,'expert'=32] {'expert'}, dimensions={0} | all-to-all | bytes 4194304 | tf_op jit(solution)/shard_map/all_to_all | solution.py:149
  317.3 7.6 %fusion.49 = f32[512,1408]{1,0:T(8,128)} fusion(bf16[512,2048]{1,0:T(8,128)(2,1)S(1)} %bitcast.105, bf16[2048,1408]{1,0:T(8,128)(2,1)} %bitcast.23), kind=kOutput, calls=%fused_computation.95 | convolution fusion | flops 2952790016 | bytes 10747904 | tf_op jit(solution)/shard_map/dot_general | solution.py:157
  324.9 6.0 %convolution_convert_fusion = bf16[512,2048]{1,0:T(8,128)(2,1)} fusion(bf16[1,2048,704]{1,2,0:T(8,128)(2,1)} %all-gather.11.cloned.1.call-done, f32[512,1408]{1,0:T(8,128)} %fusion.49), kind=kOutput, calls=%fused_computation.41 | convolution fusion | flops 1479606272 | bytes 8126464 | tf_op jit(solution)/shard_map/dot_general | solution.py:162
  330.9 5.3 %all-to-all-start.2 = ((bf16[32,16,2048]{2,1,0:T(8,128)(2,1)}), bf16[32,16,2048]{2,1,0:T(8,128)(2,1)S(1)}, u32[]{:S(2)}, u32[]{:S(2)}) async-start(bf16[32,16,2048]{2,1,0:T(8,128)(2,1)} %bitcast.103), calls=%async_computation.2 | async-start | bytes 4194304 | tf_op jit(solution)/shard_map/all_to_all | solution.py:165
  336.5 1.3 fusion.48
  338.1 44.7 %all-to-all-done.2 = bf16[32,16,2048]{2,1,0:T(8,128)(2,1)S(1)} async-done(((bf16[32,16,2048]{2,1,0:T(8,128)(2,1)}), bf16[32,16,2048]{2,1,0:T(8,128)(2,1)S(1)}, u32[]{:S(2)}, u32[]{:S(2)}) %all-to-all-start.2) | async-done | bytes 2097184 | tf_op jit(solution)/shard_map/all_to_all | solution.py:165
  382.8 3.1 gather_fusion
  385.9 3.9 reshape.158
  389.8 3.8 multiply_reduce_fusion
  393.6 0.8 fusion.35
  (70 shorter events, 6.6 us)
Async XLA Ops:
  6.5 180.3 %copy-start = (bf16[8,512,128]{2,1,0:T(8,128)(2,1)S(1)}, bf16[8,512,128]{2,1,0:T(8,128)(2,1)}, u32[]{:S(2)}) copy-start(bf16[8,512,128]{2,1,0:T(8,128)(2,1)} %param.21) | copy-start | bytes 3145732
  6.5 70.4 %all-gather.7.cloned.1.call-start = ((), (), s32[]{:S(2)}) async-start(), calls=%async_computation.4 | async-start | bytes 1392640 | tf_op jit(solution)/shard_map/all_gather | solution.py:65
  7.3 161.2 %all-gather.5.cloned.1.call-start = ((), (), s32[]{:S(2)}) async-start(), calls=%async_computation.3 | async-start | bytes 2785280 | tf_op jit(solution)/shard_map/all_gather | solution.py:66
  9.1 249.2 %all-gather.9.cloned.1.call-start = ((), (), s32[]{:S(2)}) async-start(), calls=%async_computation.5 | async-start | bytes 4325376 | tf_op jit(solution)/shard_map/all_gather | solution.py:124
  14.0 11.2 %copy-start.13 = (s32[1,64,6]{1,0,2:T(1,128)S(1)}, s32[1,64,6]{1,0,2:T(1,128)}, u32[]{:S(2)}) copy-start(s32[1,64,6]{1,0,2:T(1,128)} %param.25) | copy-start | bytes 4612
  14.0 11.6 %copy-start.8 = (bf16[1,64,4608]{2,1,0:T(8,128)(2,1)S(1)}, bf16[1,64,4608]{2,1,0:T(8,128)(2,1)}, u32[]{:S(2)}) copy-start(bf16[1,64,4608]{2,1,0:T(8,128)(2,1)} %param.16) | copy-start | bytes 1769476
  14.0 13.0 %copy-start.14 = (s32[1,4]{1,0:T(1,128)S(1)}, s32[1,4]{1,0:T(1,128)}, u32[]{:S(2)}) copy-start(s32[1,4]{1,0:T(1,128)} %param.19) | copy-start | bytes 52
  14.0 13.2 %copy-start.15 = (s32[1,4]{1,0:T(1,128)S(1)}, s32[1,4]{1,0:T(1,128)}, u32[]{:S(2)}) copy-start(s32[1,4]{1,0:T(1,128)} %param.20) | copy-start | bytes 52
  14.0 249.6 %all-to-all-start.1 = ((bf16[16,1,128,1408]{3,2,1,0:T(8,128)(2,1)}), bf16[16,1,128,1408]{3,2,1,0:T(8,128)(2,1)}, u32[]{:S(2)}, u32[]{:S(2)}) async-start(bf16[16,1,128,1408]{3,2,1,0:T(8,128)(2,1)} %stack.2), calls=%async_computation.1 | async-start | bytes 11534336 | tf_op jit(solution)/shard_map/all_to_all | solution.py:152
  24.6 300.3 %all-gather.11.cloned.1.call-start = ((), (), s32[]{:S(2)}) async-start(), calls=%async_computation.6 | async-start | bytes 3063808 | tf_op jit(solution)/shard_map/all_gather | solution.py:154
  180.2 1.7 copy-start.7
  181.2 1.4 copy-start.3
  185.4 73.0 %copy-start.10 = (bf16[1,64,2048]{2,1,0:T(8,128)(2,1)S(1)}, bf16[1,64,2048]{2,1,0:T(8,128)(2,1)}, u32[]{:S(2)}) copy-start(bf16[1,64,2048]{2,1,0:T(8,128)(2,1)} %param.15) | copy-start | bytes 786436
  187.2 75.6 %copy-start.9 = (s32[512,64]{0,1:T(8,128)S(1)}, s32[512,64]{0,1:T(8,128)}, u32[]{:S(2)}) copy-start(s32[512,64]{0,1:T(8,128)} %convert_reduce_fusion) | copy-start | bytes 393220
  187.2 75.6 %copy-start.12 = (f32[2048]{0:T(1024)S(1)}, f32[2048]{0:T(1024)}, u32[]{:S(2)}) copy-start(f32[2048]{0:T(1024)} %param.23) | copy-start | bytes 24580
  262.0 0.8 copy-start.5
  330.9 5.6 %copy-start.11 = (bf16[2048,32]{0,1:T(8,128)(2,1)S(1)}, bf16[2048,32]{0,1:T(8,128)(2,1)}, u32[]{:S(2)}) copy-start(bf16[2048,32]{0,1:T(8,128)(2,1)} %param.24) | copy-start | bytes 393220
  330.9 51.9 %all-to-all-start.2 = ((bf16[32,16,2048]{2,1,0:T(8,128)(2,1)}), bf16[32,16,2048]{2,1,0:T(8,128)(2,1)S(1)}, u32[]{:S(2)}, u32[]{:S(2)}) async-start(bf16[32,16,2048]{2,1,0:T(8,128)(2,1)} %bitcast.103), calls=%async_computation.2 | async-start | bytes 4194304 | tf_op jit(solution)/shard_map/all_to_all | solution.py:165
  389.8 3.8 copy-start.6
Sparse Core Ops, SparseCore 0:
  9.5 67.3 all-gather.6
  79.0 89.3 all-gather.4
  171.6 86.6 all-gather.8
  260.2 44.3 all-gather.10
